TPU v7x, 32 devices: a whole 2x2x4 slice. The times are simulated.
32 devices in a mesh: row: 4 (over y, core), col: 8 (over z, x).
Axes of the slice: x: 2, y: 2, z: 4, core: 2. Of those that a mesh axis runs over, the one named last changes fastest.
Arguments:
- node_feats: bfloat16 [8192, 256], P(('row', 'col')), may hold values from -6 to 6
- weight: bfloat16 [256, 256], replicated, may hold values from -0.375 to 0.375
- cotangent: bfloat16 [8192, 256], P(('row', 'col')), may hold values from -6 to 6
- band_tiles: bfloat16 [384, 128, 128], P(('row', 'col')), may hold values from 0 to 0.049804688
- band_coords: int32 [384, 2], P(('row', 'col')), may hold values from 0 to 5, as said below
- bound_tiles: bfloat16 [1280, 128, 128], P(('row', 'col')), may hold values from 0 to 0.049804688
- bound_coords: int32 [1280, 2], P(('row', 'col')), may hold values from 0 to 7, as said below
- bound_count: int32 [32], P(('row', 'col')), may hold values from 0 to 40, as said below
- recv_lists: int32 [32, 8], P(('row', 'col')), may hold values from -1 to 1, as said below
- send_lists: int32 [32, 8], P(('row', 'col')), may hold values from -1 to 1, as said below
- reorder: int32 [32, 256], P(('row', 'col')), may hold values from 0 to 255, each once within a row
Outputs:
- node_out: bfloat16 [8192, 256], P(('row', 'col'))
- feat_grad: bfloat16 [8192, 256], P(('row', 'col'))
- weight_grad: float32 [256, 256], replicated
Inputs may be any that keep to these rules, and one draw needn't show every extreme that they name: recv_lists[r * 8 + c, s] is a row block of device r * 8 + s, below 2, or -1 for none; it is -1 where s = c. In every row group one device receives a block from every other column. send_lists[r * 8 + s, c] equals recv_lists[r * 8 + c, s]. bound_count[d] is at least the number of entries of recv_lists[d] that are not -1; in every row group one device has all 40 slots live. `bound_coords`: pairs (row block below 2, owner column below 8); for k < bound_count[d] the owner column s of slot k has recv_lists[d, s] >= 0, and every such column is named by one of them; slots from bound_count[d] on are not used. `band_coords`: pairs (row block below 2, extended column block below (768) / 128); no pair twice on one device. `reorder`: each row is a permutation.
All inputs are finite; a program needn't handle non-finite values.
Results may differ from a plain program's by a relative error of at most 0.0095.
Values may be sent and summed in bfloat16 or wider, within the bound.
No kernel may reach another device: no remote copies, remote signals or barrier semaphores. Data moves between devices by JAX's collectives and lax.ppermute only.
A program may use at most 64 MiB of HBM per device.

v0:
```python
import jax
import jax.numpy as jnp
from jax import lax
from jax.sharding import PartitionSpec as P

BW = 256


def padded_2(cells, sides, width):
    for axis, dim in sides:
        count = lax.axis_size(axis)
        head = lax.slice_in_dim(cells, 0, width, axis=dim)
        tail = lax.slice_in_dim(cells, cells.shape[dim] - width, cells.shape[dim], axis=dim)
        cells = jnp.concatenate(
            [
                lax.ppermute(tail, axis, [(i, (i + 1) % count) for i in range(count)]),
                cells,
                lax.ppermute(head, axis, [((i + 1) % count, i) for i in range(count)]),
            ],
            axis=dim,
        )
    return cells


def split_sum(selector, terms):
    high_part = terms.astype(jnp.bfloat16)
    low_part = (terms - high_part.astype(jnp.float32)).astype(jnp.bfloat16)
    pick = selector.astype(jnp.bfloat16)
    upper_sum = jnp.einsum("rk,kaf->raf", pick, high_part, preferred_element_type=jnp.float32)
    lower_sum = jnp.einsum("rk,kaf->raf", pick, low_part, preferred_element_type=jnp.float32)
    return upper_sum + lower_sum


def on_device(
    node_feats,
    weight,
    cotangent,
    band_tiles,
    band_coords,
    bound_tiles,
    bound_coords,
    bound_count,
    recv_lists,
    send_lists,
    reorder,
):
    tile_size = band_tiles.shape[1]
    row_count = node_feats.shape[0]
    width_feat = node_feats.shape[1]
    tile_rows = row_count // tile_size
    rim_tiles = BW // tile_size
    col_tiles = tile_rows + 2 * rim_tiles
    ext_count = row_count + 2 * BW
    peers = lax.axis_size("col")
    slot_total = bound_tiles.shape[0]
    order = reorder[0]
    inverse = (
        jnp.zeros((row_count,), jnp.int32).at[order].set(jnp.arange(row_count, dtype=jnp.int32))
    )
    x_band = jnp.take(node_feats, order, axis=0)
    hidden = jnp.dot(x_band, weight, preferred_element_type=jnp.float32).astype(jnp.bfloat16)
    band_row_ids = band_coords[:, 0]
    band_col_ids = band_coords[:, 1]
    band_dense = jnp.zeros((tile_rows, tile_size, col_tiles, tile_size), jnp.bfloat16)
    band_dense = (
        band_dense.at[band_row_ids, :, band_col_ids].set(band_tiles).reshape(row_count, ext_count)
    )
    extended = padded_2(hidden, (("row", 0),), BW)
    mixed = jnp.dot(band_dense, extended, preferred_element_type=jnp.float32)
    blocks = hidden.reshape(tile_rows, tile_size, width_feat)
    giving = send_lists[0]
    outgoing = jnp.where(
        (giving >= 0)[:, None, None],
        jnp.take(blocks, jnp.maximum(giving, 0), axis=0),
        jnp.zeros((), jnp.bfloat16),
    )
    arrived = lax.all_to_all(outgoing, "col", split_axis=0, concat_axis=0, tiled=True)
    tile_range = jnp.arange(tile_rows, dtype=jnp.int32)
    live_slots = jnp.arange(slot_total, dtype=jnp.int32) < bound_count[0]
    bound_row_ids = bound_coords[:, 0]
    bound_owner = bound_coords[:, 1]
    bound_onehot = (bound_row_ids[None, :] == tile_range[:, None]) & live_slots[None, :]
    slot_rows = jnp.take(arrived, bound_owner, axis=0).reshape(slot_total * tile_size, width_feat)
    placed = jnp.einsum(
        "rk,kab->rakb",
        bound_onehot.astype(jnp.bfloat16),
        bound_tiles,
        preferred_element_type=jnp.bfloat16,
    )
    placed = placed.reshape(row_count, slot_total * tile_size)
    mixed = mixed + jnp.dot(placed, slot_rows, preferred_element_type=jnp.float32)
    out_band = jax.nn.silu(mixed).astype(jnp.bfloat16)
    node_out = jnp.take(out_band, inverse, axis=0)
    grad_band = jnp.take(cotangent, order, axis=0).astype(jnp.float32)
    sigma = jax.nn.sigmoid(mixed)
    slope = (grad_band * sigma * (1.0 + mixed * (1.0 - sigma))).astype(jnp.bfloat16)
    slope_blocks = slope.reshape(tile_rows, tile_size, width_feat)
    ext_grad = lax.dot_general(
        band_dense, slope, (((0,), (0,)), ((), ())), preferred_element_type=jnp.float32
    )
    rim_terms = jnp.concatenate([ext_grad[:BW], ext_grad[BW + row_count :]], axis=0).astype(
        jnp.bfloat16
    )
    padded = padded_2(rim_terms, (("row", 0),), BW)
    grad_hidden = ext_grad[BW : BW + row_count]
    grad_hidden = grad_hidden.at[:BW].add(padded[:BW].astype(jnp.float32))
    grad_hidden = grad_hidden.at[row_count - BW :].add(padded[3 * BW :].astype(jnp.float32))
    slot_back = jnp.einsum(
        "kab,kaf->kbf",
        bound_tiles,
        jnp.take(slope_blocks, bound_row_ids, axis=0),
        preferred_element_type=jnp.float32,
    )
    owner_range = jnp.arange(peers, dtype=jnp.int32)
    owner_onehot = (bound_owner[None, :] == owner_range[:, None]) & live_slots[None, :]
    to_owner = split_sum(owner_onehot, slot_back).astype(jnp.bfloat16)
    returned = lax.all_to_all(to_owner, "col", split_axis=0, concat_axis=0, tiled=True)
    block_onehot = (giving[None, :] == tile_range[:, None]).astype(jnp.bfloat16)
    from_peers = jnp.einsum(
        "bs,saf->baf", block_onehot, returned, preferred_element_type=jnp.float32
    )
    grad_hidden = grad_hidden + from_peers.reshape(row_count, width_feat)
    grad_round = grad_hidden.astype(jnp.bfloat16)
    partial_weight = lax.dot_general(
        x_band, grad_round, (((0,), (0,)), ((), ())), preferred_element_type=jnp.float32
    )
    nodes_all = row_count * lax.axis_size("row") * peers
    weight_grad = lax.psum(partial_weight, ("row", "col")) * nodes_all ** (-0.5)
    feat_band = lax.dot_general(
        grad_round, weight, (((1,), (1,)), ((), ())), preferred_element_type=jnp.float32
    ).astype(jnp.bfloat16)
    feat_grad = jnp.take(feat_band, inverse, axis=0)
    return (node_out, feat_grad, weight_grad)


def solution(mesh):
    in_specs = (
        P(("row", "col"), None),
        P(),
        P(("row", "col"), None),
        P(("row", "col"), None, None),
        P(("row", "col"), None),
        P(("row", "col"), None, None),
        P(("row", "col"), None),
        P(("row", "col")),
        P(("row", "col"), None),
        P(("row", "col"), None),
        P(("row", "col"), None),
    )
    out_specs = (P(("row", "col"), None), P(("row", "col"), None), P())
    return jax.shard_map(
        on_device, mesh=mesh, in_specs=in_specs, out_specs=out_specs, check_vma=False
    )
```

profile of v0, /device:TPU:0, one launch (start us, length us, event | category | flops | bytes accessed | tf_op | source)
XLA Modules:
  0.0 214.7 jit_solution(14946147041477789685)
XLA Ops:
  7.2 0.8 compare_select_fusion.2
  8.0 0.7 compare_and_fusion.1
  8.7 1.9 gather_fusion.3
  11.4 2.0 collective-permute-start.1
  15.3 0.9 select_select_fusion
  16.3 6.5 %all-to-all-start = ((bf16[8,128,256]{2,1,0:T(8,128)(2,1)}), bf16[8,128,256]{2,1,0:T(8,128)(2,1)S(1)}, u32[]{:S(2)}, u32[]{:S(2)}) async-start(bf16[8,128,256]{2,1,0:T(8,128)(2,1)} %select_select_fusion), calls=%async_computation | async-start | bytes 1048576 | tf_op jit(solution)/shard_map/all_to_all | solution.py:77
  25.2 0.8 copy.20
  26.1 1.8 gather_fusion.5
  28.0 2.0 scatter_fusion
  30.1 1.1 copy.19
  31.2 2.1 scatter_custom_fusion.1
  33.8 1.7 broadcast_multiply_fusion
  35.6 1.8 all-to-all-done
  37.3 0.7 gather_fusion.1
  38.4 1.4 copy-done.4
  39.8 0.8 fusion.1
  40.8 1.3 multiply_convert_fusion
  42.2 2.4 %gather_fusion.2 = bf16[40,128,256]{2,1,0:T(8,128)(2,1)} fusion(bf16[2,128,256]{2,1,0:T(8,128)(2,1)S(1)} %bitcast.73, s32[1024]{0:T(1024)S(1)} %pad_clamp_fusion), kind=kCustom, calls=%fused_computation.6 | custom fusion | bytes 5243040 | tf_op jit(solution)/shard_map/jit(_take)/gather | solution.py:111
  44.6 4.9 %fusion = (bf16[40,128,256]{1,2,0:T(8,128)(2,1)S(1)}, bf16[40,128,256]{1,2,0:T(8,128)(2,1)}) fusion(bf16[40,128,128]{2,1,0:T(8,128)(2,1)} %param.26, bf16[40,128,256]{2,1,0:T(8,128)(2,1)} %gather_fusion.2, pred[40]{0:T(512)(128)(4,1)S(1)} %copy-done.16), kind=kOutput, calls=%fused_computation.11 | convolution fusion | flops 342097920 | bytes 9175080 | tf_op jit(solution)/shard_map/kab,kaf->kbf/dot_general | solution.py:108
  49.5 4.7 %copy.22 = bf16[40,128,256]{2,0,1:T(8,128)(2,1)} copy(bf16[40,128,256]{1,2,0:T(8,128)(2,1)} %get-tuple-element.45) | data formatting | bytes 5242880 | tf_op jit(solution)/shard_map/convert_element_type | solution.py:26
  54.2 3.4 %copy.23 = bf16[40,128,256]{2,0,1:T(8,128)(2,1)} copy(bf16[40,128,256]{1,2,0:T(8,128)(2,1)S(1)} %get-tuple-element.44) | data formatting | bytes 5242880 | tf_op jit(solution)/shard_map/convert_element_type | solution.py:27
  57.6 2.5 %fusion.28 = f32[8,128,256]{2,0,1:T(8,128)S(1)} fusion(bf16[40,128,256]{2,0,1:T(8,128)(2,1)} %copy.22, s32[40]{0:T(128)S(1)} %get-tuple-element.50, pred[40]{0:T(512)(128)(4,1)S(1)} %copy-done.15), kind=kOutput, calls=%fused_computation.62 | convolution fusion | flops 20972160 | bytes 3670216 | tf_op jit(solution)/shard_map/rk,kaf->raf/dot_general | solution.py:29
  60.7 0.9 copy.24
  61.6 4.2 %all-to-all-start.1 = ((bf16[8,128,256]{2,1,0:T(8,128)(2,1)}), bf16[8,128,256]{2,1,0:T(8,128)(2,1)S(1)}, u32[]{:S(2)}, u32[]{:S(2)}) async-start(bf16[8,128,256]{2,1,0:T(8,128)(2,1)} %copy.24), calls=%async_computation.1 | async-start | bytes 1048576 | tf_op jit(solution)/shard_map/all_to_all | solution.py:117
  66.3 1.7 collective-permute-start.3
  68.0 1.1 gather_fusion.4
  69.2 10.8 %all-to-all-done.1 = bf16[8,128,256]{2,1,0:T(8,128)(2,1)S(1)} async-done(((bf16[8,128,256]{2,1,0:T(8,128)(2,1)}), bf16[8,128,256]{2,1,0:T(8,128)(2,1)S(1)}, u32[]{:S(2)}, u32[]{:S(2)}) %all-to-all-start.1) | async-done | bytes 524320 | tf_op jit(solution)/shard_map/all_to_all | solution.py:117
  80.7 1.0 fusion.24
  81.7 1.1 gather_fusion.6
  82.9 0.8 broadcast_select_fusion.1
  83.7 122.5 %all-reduce.2.cloned.1.call-done = f32[256,256]{1,0:T(8,128)} async-done(((f32[256,256]{1,0:T(8,128)}), f32[256,256]{1,0:T(8,128)}) %all-reduce.2.cloned.1.call-update) | async-done | bytes 262160 | tf_op jit(solution)/shard_map/psum | solution.py:128
  206.1 1.7 broadcast_multiply_fusion.1
  (78 shorter events, 7.3 us)
Async XLA Ops:
  7.2 3.4 %copy-start = (bf16[256,256]{1,0:T(8,128)(2,1)S(1)}, bf16[256,256]{1,0:T(8,128)(2,1)}, u32[]{:S(2)}) copy-start(bf16[256,256]{1,0:T(8,128)(2,1)} %param.22) | copy-start | bytes 393220
  7.2 15.6 %copy-start.11 = (s32[1,256]{1,0:T(1,128)S(1)}, s32[1,256]{1,0:T(1,128)}, u32[]{:S(2)}) copy-start(s32[1,256]{1,0:T(1,128)} %param.30) | copy-start | bytes 3076
  7.2 16.2 %copy-start.9 = (s32[40,2]{0,1:T(2,128)S(1)}, s32[40,2]{0,1:T(2,128)}, u32[]{:S(2)}) copy-start(s32[40,2]{0,1:T(2,128)} %param.27) | copy-start | bytes 964
  7.2 17.4 %copy-start.21 = (s32[12,2]{0,1:T(2,128)S(1)}, s32[12,2]{0,1:T(2,128)}, u32[]{:S(2)}) copy-start(s32[12,2]{0,1:T(2,128)} %param.25) | copy-start | bytes 292
  7.2 18.0 %copy-start.3 = (bf16[40,128,128]{2,1,0:T(8,128)(2,1)S(1)}, bf16[40,128,128]{2,1,0:T(8,128)(2,1)}, u32[]{:S(2)}) copy-start(bf16[40,128,128]{2,1,0:T(8,128)(2,1)} %param.26) | copy-start | bytes 3932164
  8.7 5.3 %copy-start.12 = (pred[256]{0:T(512)(128)(4,1)}, pred[256]{0:T(512)(128)(4,1)S(1)}, u32[]{:S(2)}) copy-start(pred[256]{0:T(512)(128)(4,1)S(1)} %compare_and_fusion.1) | copy-start | bytes 772
  10.6 4.1 %copy-start.6 = (bf16[256,256]{1,0:T(8,128)(2,1)}, bf16[256,256]{1,0:T(8,128)(2,1)S(1)}, u32[]{:S(2)}) copy-start(bf16[256,256]{1,0:T(8,128)(2,1)S(1)} %gather_fusion.3) | copy-start | bytes 393220
  10.9 29.8 %collective-permute-start = (bf16[256,256]{1,0:T(8,128)(2,1)S(1)}, bf16[256,256]{1,0:T(8,128)(2,1)}, u32[]{:S(2)}, u32[]{:S(2)}) collective-permute-start(bf16[256,256]{1,0:T(8,128)(2,1)S(1)} %convolution_convert_fusion.1), channel_id=1, source_target_pairs={{0,8},{8,16},{16,24},{24,0},{1,9},{9,17},{17,25},{25,1},{2,10},{10... | collective-permute-start | bytes 393224 | tf_op jit(solution)/shard_map/ppermute | solution.py:16
  11.4 29.3 %collective-permute-start.1 = (bf16[256,256]{1,0:T(8,128)(2,1)S(1)}, bf16[256,256]{1,0:T(8,128)(2,1)}, u32[]{:S(2)}, u32[]{:S(2)}) collective-permute-start(bf16[256,256]{1,0:T(8,128)(2,1)S(1)} %convolution_convert_fusion.1), channel_id=1, source_target_pairs={{8,0},{16,8},{24,16},{0,24},{9,1},{17,9},{25,17},{1,25},{10,2},{18... | collective-permute-start | bytes 393224 | tf_op jit(solution)/shard_map/ppermute | solution.py:18
  15.3 10.8 %copy-start.2 = (bf16[256,256]{1,0:T(8,128)(2,1)S(1)}, bf16[256,256]{1,0:T(8,128)(2,1)}, u32[]{:S(2)}) copy-start(bf16[256,256]{1,0:T(8,128)(2,1)} %param.23) | copy-start | bytes 393220
  16.3 21.1 %all-to-all-start = ((bf16[8,128,256]{2,1,0:T(8,128)(2,1)}), bf16[8,128,256]{2,1,0:T(8,128)(2,1)S(1)}, u32[]{:S(2)}, u32[]{:S(2)}) async-start(bf16[8,128,256]{2,1,0:T(8,128)(2,1)} %select_select_fusion), calls=%async_computation | async-start | bytes 1048576 | tf_op jit(solution)/shard_map/all_to_all | solution.py:77
  26.1 7.2 %copy-start.17 = (s32[40]{0:T(128)S(1)}, s32[40]{0:T(128)}, u32[]{:S(2)}) copy-start(s32[40]{0:T(128)} %get-tuple-element.51) | copy-start | bytes 484
  26.1 7.2 %copy-start.14 = (pred[40]{0:T(512)(128)(4,1)S(1)}, pred[40]{0:T(512)(128)(4,1)}, u32[]{:S(2)}) copy-start(pred[40]{0:T(512)(128)(4,1)} %iota_compare_fusion.1) | copy-start | bytes 124
  26.1 7.2 %copy-start.19 = (s32[40]{0:T(128)S(1)}, s32[40]{0:T(128)}, u32[]{:S(2)}) copy-start(s32[40]{0:T(128)} %get-tuple-element.53) | copy-start | bytes 484
  26.1 7.2 %copy-start.10 = (s32[40,2]{0,1:T(2,128)S(1)}, s32[40,2]{0,1:T(2,128)}, u32[]{:S(2)}) copy-start(s32[40,2]{0,1:T(2,128)} %param.27) | copy-start | bytes 964
  38.1 1.7 copy-start.4
  39.8 1.0 copy-start.5
  39.8 1.0 copy-start.8
  39.8 1.0 copy-start.13
  42.2 2.4 %copy-start.16 = (pred[40]{0:T(512)(128)(4,1)S(1)}, pred[40]{0:T(512)(128)(4,1)}, u32[]{:S(2)}) copy-start(pred[40]{0:T(512)(128)(4,1)} %get-tuple-element.54) | copy-start | bytes 124
  54.2 3.4 %copy-start.15 = (pred[40]{0:T(512)(128)(4,1)S(1)}, pred[40]{0:T(512)(128)(4,1)}, u32[]{:S(2)}) copy-start(pred[40]{0:T(512)(128)(4,1)} %iota_compare_fusion.1) | copy-start | bytes 124
  57.6 2.5 %copy-start.1 = (bf16[40,128,256]{2,0,1:T(8,128)(2,1)S(1)}, bf16[40,128,256]{2,0,1:T(8,128)(2,1)}, u32[]{:S(2)}) copy-start(bf16[40,128,256]{2,0,1:T(8,128)(2,1)} %copy.23) | copy-start | bytes 7864324
  60.1 5.8 %copy-start.18 = (s32[256]{0:T(256)S(1)}, s32[256]{0:T(256)}, u32[]{:S(2)}) copy-start(s32[256]{0:T(256)} %scatter_custom_fusion.1) | copy-start | bytes 3076
  60.7 19.3 %copy-start.20 = (s32[1,8]{1,0:T(1,128)S(1)}, s32[1,8]{1,0:T(1,128)}, u32[]{:S(2)}) copy-start(s32[1,8]{1,0:T(1,128)} %param.29) | copy-start | bytes 100
  61.6 18.4 %all-to-all-start.1 = ((bf16[8,128,256]{2,1,0:T(8,128)(2,1)}), bf16[8,128,256]{2,1,0:T(8,128)(2,1)S(1)}, u32[]{:S(2)}, u32[]{:S(2)}) async-start(bf16[8,128,256]{2,1,0:T(8,128)(2,1)} %copy.24), calls=%async_computation.1 | async-start | bytes 1048576 | tf_op jit(solution)/shard_map/all_to_all | solution.py:117
  65.8 140.3 %all-reduce.2.cloned.1.call-start = ((), (), s32[]{:S(2)}) async-start(), calls=%async_computation.2 | async-start | bytes 524288 | tf_op jit(solution)/shard_map/psum | solution.py:128
  65.9 14.8 %copy-start.7 = (bf16[256,256]{1,0:T(8,128)(2,1)S(1)}, bf16[256,256]{1,0:T(8,128)(2,1)}, u32[]{:S(2)}) copy-start(bf16[256,256]{1,0:T(8,128)(2,1)} %copy-done.6) | copy-start | bytes 393220
  66.2 14.1 %collective-permute-start.2 = (bf16[256,256]{1,0:T(8,128)(2,1)S(1)}, bf16[256,256]{1,0:T(8,128)(2,1)S(1)}, u32[]{:S(2)}, u32[]{:S(2)}) collective-permute-start(bf16[256,256]{1,0:T(8,128)(2,1)S(1)} %get-tuple-element.46), channel_id=1, source_target_pairs={{0,8},{8,16},{16,24},{24,0},{1,9},{9,17},{17,25},{25,1},{2,10},{10... | collective-permute-start | bytes 393224 | tf_op jit(solution)/shard_map/ppermute | solution.py:16
  66.3 14.1 %collective-permute-start.3 = (bf16[256,256]{1,0:T(8,128)(2,1)S(1)}, bf16[256,256]{1,0:T(8,128)(2,1)S(1)}, u32[]{:S(2)}, u32[]{:S(2)}) collective-permute-start(bf16[256,256]{1,0:T(8,128)(2,1)S(1)} %get-tuple-element.47), channel_id=1, source_target_pairs={{8,0},{16,8},{24,16},{0,24},{9,1},{17,9},{25,17},{1,25},{10,2},{18... | collective-permute-start | bytes 393224 | tf_op jit(solution)/shard_map/ppermute | solution.py:18
Sparse Core Ops, SparseCore 0:
  83.0 123.1 all-reduce.1
where the time goes:
time: 215 us
  waiting for transfers between devices  135 us (63%)
  local copies, waits for them, and re-layouts  26.5 us (12%)
  starting transfers between devices  15.1 us (7%)
  between operations  15.1 us (7%)
  matrix products  12.3 us (6%)
  other arithmetic  10.6 us (5%)
    psum x1, waiting for transfers between devices, on_device(): weight_grad = lax.psum(partial_weight, ('row', 'col')) * nodes_all ** (-0.5)  122 us
    all_to_all x1, waiting for transfers between devices, on_device(): lax.all_to_all(to_owner, 'col', split_axis=0, concat_axis=0, tiled=True)  10.8 us
    all_to_all x1, starting transfers between devices, on_device(): lax.all_to_all(outgoing, 'col', split_axis=0, concat_axis=0, tiled=True)  6.53 us
    dot_general x1, matrix products, on_device(): jnp.einsum('kab,kaf->kbf', bound_tiles, jnp.take(slope_blocks, bound_row_...  4.94 us
    convert_element_type x1, local copies, waits for them, and re-layouts, split_sum(): high_part = terms.astype(jnp.bfloat16)  4.69 us
  transfers between devices with their start and end apart: 7, of which 3 were waited for; matrix products, arithmetic and copies ran while one was open for 9% of the time, Pallas kernels for 0%

commit v1 on v0

--- a/solution.py
+++ b/solution.py
@@ -125,7 +125,7 @@
         x_band, grad_round, (((0,), (0,)), ((), ())), preferred_element_type=jnp.float32
     )
     nodes_all = row_count * lax.axis_size("row") * peers
-    weight_grad = lax.psum(partial_weight, ("row", "col")) * nodes_all ** (-0.5)
+    weight_grad = lax.psum(lax.psum(partial_weight, "col"), "row") * nodes_all ** (-0.5)
     feat_band = lax.dot_general(
         grad_round, weight, (((1,), (1,)), ((), ())), preferred_element_type=jnp.float32
     ).astype(jnp.bfloat16)

time: 215 us -> 193 us (0.90)
  waiting for transfers between devices: 135 us -> 113 us
    psum x1 -> x2, waiting for transfers between devices: 122 us -> 99.1 us  [the longest x1 66.3 us: on_device(): lax.psum(partial_weight, 'col')]
  transfers between devices with their start and end apart: 7 -> 8, of which waited for: 3 -> 4; matrix products, arithmetic and copies ran while one was open for 9% -> 11% of each run, Pallas kernels for 0% -> 0%
where the time goes in v1:
time: 193 us
  waiting for transfers between devices  113 us (59%)
  local copies, waits for them, and re-layouts  26.5 us (14%)
  starting transfers between devices  15.3 us (8%)
  between operations  15.1 us (8%)
  matrix products  12.3 us (6%)
  other arithmetic  10.6 us (5%)
    psum x1, waiting for transfers between devices, on_device(): lax.psum(partial_weight, 'col')  66.3 us
    psum x1, waiting for transfers between devices, on_device(): lax.psum(lax.psum(partial_weight, 'col'), 'row') * nodes_all ** (-0.5)  32.9 us
    all_to_all x1, waiting for transfers between devices, on_device(): lax.all_to_all(to_owner, 'col', split_axis=0, concat_axis=0, tiled=True)  11.9 us
    all_to_all x1, starting transfers between devices, on_device(): lax.all_to_all(outgoing, 'col', split_axis=0, concat_axis=0, tiled=True)  6.53 us
    dot_general x1, matrix products, on_device(): jnp.einsum('kab,kaf->kbf', bound_tiles, jnp.take(slope_blocks, bound_row_...  4.94 us
    convert_element_type x1, local copies, waits for them, and re-layouts, split_sum(): high_part = terms.astype(jnp.bfloat16)  4.69 us
    all_to_all x1, starting transfers between devices, on_device(): lax.all_to_all(to_owner, 'col', split_axis=0, concat_axis=0, tiled=True)  4.37 us
  transfers between devices with their start and end apart: 8, of which 4 were waited for; matrix products, arithmetic and copies ran while one was open for 11% of the time, Pallas kernels for 0%

profile of v1, /device:TPU:0, one launch (start us, length us, event | category | flops | bytes accessed | tf_op | source)
XLA Modules:
  0.0 192.7 jit_solution(15419963762835371703)
XLA Ops:
  7.2 0.8 compare_select_fusion.2
  8.7 1.9 gather_fusion.3
  11.4 2.0 %collective-permute-start.1 = (bf16[256,256]{1,0:T(8,128)(2,1)S(1)}, bf16[256,256]{1,0:T(8,128)(2,1)}, u32[]{:S(2)}, u32[]{:S(2)}) collective-permute-start(bf16[256,256]{1,0:T(8,128)(2,1)S(1)} %convolution_convert_fusion.1), channel_id=1, source_target_pairs={{8,0},{16,8},{24,16},{0,24},{9,1},{17,9},{25,17},{1,25},{10,2},{18... | collective-permute-start | bytes 393224 | tf_op jit(solution)/shard_map/ppermute | solution.py:18
  15.3 0.9 select_select_fusion
  16.3 6.5 %all-to-all-start = ((bf16[8,128,256]{2,1,0:T(8,128)(2,1)}), bf16[8,128,256]{2,1,0:T(8,128)(2,1)S(1)}, u32[]{:S(2)}, u32[]{:S(2)}) async-start(bf16[8,128,256]{2,1,0:T(8,128)(2,1)} %select_select_fusion), calls=%async_computation | async-start | bytes 1048576 | tf_op jit(solution)/shard_map/all_to_all | solution.py:77
  25.2 0.8 copy.20
  26.1 1.8 gather_fusion.5
  28.0 2.0 %scatter_fusion = bf16[2,128,6,128]{3,1,2,0:T(8,128)(2,1)S(1)} fusion(bf16[2,128,6,128]{3,1,2,0:T(8,128)(2,1)S(1)} %broadcast_in_dim.61, s32[12]{0:T(128)S(1)} %fusion.42, bf16[12,128,128]{2,1,0:T(8,128)(2,1)} %param.24), kind=kCustom, calls=%fused_computation.7 | custom fusion | bytes 1179744 | tf_op jit(solution)/shard_map/scatter | solution.py:66
  30.1 1.1 copy.19
  31.2 2.1 %scatter_custom_fusion.1 = s32[256]{0:T(256)} fusion(s32[256]{0:T(256)} %bitcast.81, s32[256]{0:T(256)S(1)} %iota.18, s32[]{:T(128)} %constant.131.clone.1), kind=kCustom, calls=%fused_computation.85 | custom fusion | bytes 1536 | tf_op jit(solution)/shard_map/scatter | solution.py:58
  33.8 1.7 broadcast_multiply_fusion
  35.6 1.8 all-to-all-done
  37.3 0.7 gather_fusion.1
  38.4 1.4 copy-done.4
  39.8 0.8 fusion.1
  40.8 1.3 multiply_convert_fusion
  42.2 2.4 %gather_fusion.2 = bf16[40,128,256]{2,1,0:T(8,128)(2,1)} fusion(bf16[2,128,256]{2,1,0:T(8,128)(2,1)S(1)} %bitcast.73, s32[1024]{0:T(1024)S(1)} %pad_clamp_fusion), kind=kCustom, calls=%fused_computation.6 | custom fusion | bytes 5243040 | tf_op jit(solution)/shard_map/jit(_take)/gather | solution.py:111
  44.6 4.9 %fusion = (bf16[40,128,256]{1,2,0:T(8,128)(2,1)S(1)}, bf16[40,128,256]{1,2,0:T(8,128)(2,1)}) fusion(bf16[40,128,128]{2,1,0:T(8,128)(2,1)} %param.26, bf16[40,128,256]{2,1,0:T(8,128)(2,1)} %gather_fusion.2, pred[40]{0:T(512)(128)(4,1)S(1)} %copy-done.16), kind=kOutput, calls=%fused_computation.11 | convolution fusion | flops 342097920 | bytes 9175080 | tf_op jit(solution)/shard_map/kab,kaf->kbf/dot_general | solution.py:108
  49.5 4.7 %copy.22 = bf16[40,128,256]{2,0,1:T(8,128)(2,1)} copy(bf16[40,128,256]{1,2,0:T(8,128)(2,1)} %get-tuple-element.45) | data formatting | bytes 5242880 | tf_op jit(solution)/shard_map/convert_element_type | solution.py:26
  54.2 3.4 %copy.23 = bf16[40,128,256]{2,0,1:T(8,128)(2,1)} copy(bf16[40,128,256]{1,2,0:T(8,128)(2,1)S(1)} %get-tuple-element.44) | data formatting | bytes 5242880 | tf_op jit(solution)/shard_map/convert_element_type | solution.py:27
  57.6 2.5 %fusion.28 = f32[8,128,256]{2,0,1:T(8,128)S(1)} fusion(bf16[40,128,256]{2,0,1:T(8,128)(2,1)} %copy.22, s32[40]{0:T(128)S(1)} %get-tuple-element.50, pred[40]{0:T(512)(128)(4,1)S(1)} %copy-done.15), kind=kOutput, calls=%fused_computation.62 | convolution fusion | flops 20972160 | bytes 3670216 | tf_op jit(solution)/shard_map/rk,kaf->raf/dot_general | solution.py:29
  60.7 0.9 copy.24
  61.6 4.4 %all-to-all-start.1 = ((bf16[8,128,256]{2,1,0:T(8,128)(2,1)}), bf16[8,128,256]{2,1,0:T(8,128)(2,1)S(1)}, u32[]{:S(2)}, u32[]{:S(2)}) async-start(bf16[8,128,256]{2,1,0:T(8,128)(2,1)} %copy.24), calls=%async_computation.1 | async-start | bytes 1048576 | tf_op jit(solution)/shard_map/all_to_all | solution.py:117
  66.4 1.7 collective-permute-start.3
  68.1 11.9 %all-to-all-done.1 = bf16[8,128,256]{2,1,0:T(8,128)(2,1)S(1)} async-done(((bf16[8,128,256]{2,1,0:T(8,128)(2,1)}), bf16[8,128,256]{2,1,0:T(8,128)(2,1)S(1)}, u32[]{:S(2)}, u32[]{:S(2)}) %all-to-all-start.1) | async-done | bytes 524320 | tf_op jit(solution)/shard_map/all_to_all | solution.py:117
  80.6 1.0 fusion.24
  81.7 1.2 gather_fusion.4
  83.1 1.2 gather_fusion.6
  84.2 66.3 %all-reduce.3.cloned.1.call-done = f32[256,256]{1,0:T(8,128)} async-done(((f32[256,256]{1,0:T(8,128)}), f32[256,256]{1,0:T(8,128)}) %all-reduce.3.cloned.1.call-update) | async-done | bytes 262160 | tf_op jit(solution)/shard_map/psum | solution.py:128
  150.5 0.8 broadcast_select_fusion.1
  151.3 32.9 %all-reduce.5.cloned.1.call-done = f32[256,256]{1,0:T(8,128)} async-done(((f32[256,256]{1,0:T(8,128)}), f32[256,256]{1,0:T(8,128)}) %all-reduce.5.cloned.1.call-update) | async-done | bytes 262160 | tf_op jit(solution)/shard_map/psum | solution.py:128
  184.2 1.7 broadcast_multiply_fusion.1
  (81 shorter events, 8.0 us)
Async XLA Ops:
  7.2 3.4 %copy-start = (bf16[256,256]{1,0:T(8,128)(2,1)S(1)}, bf16[256,256]{1,0:T(8,128)(2,1)}, u32[]{:S(2)}) copy-start(bf16[256,256]{1,0:T(8,128)(2,1)} %param.22) | copy-start | bytes 393220
  7.2 15.6 %copy-start.11 = (s32[1,256]{1,0:T(1,128)S(1)}, s32[1,256]{1,0:T(1,128)}, u32[]{:S(2)}) copy-start(s32[1,256]{1,0:T(1,128)} %param.30) | copy-start | bytes 3076
  7.2 16.2 %copy-start.9 = (s32[40,2]{0,1:T(2,128)S(1)}, s32[40,2]{0,1:T(2,128)}, u32[]{:S(2)}) copy-start(s32[40,2]{0,1:T(2,128)} %param.27) | copy-start | bytes 964
  7.2 17.4 %copy-start.21 = (s32[12,2]{0,1:T(2,128)S(1)}, s32[12,2]{0,1:T(2,128)}, u32[]{:S(2)}) copy-start(s32[12,2]{0,1:T(2,128)} %param.25) | copy-start | bytes 292
  7.2 18.0 %copy-start.3 = (bf16[40,128,128]{2,1,0:T(8,128)(2,1)S(1)}, bf16[40,128,128]{2,1,0:T(8,128)(2,1)}, u32[]{:S(2)}) copy-start(bf16[40,128,128]{2,1,0:T(8,128)(2,1)} %param.26) | copy-start | bytes 3932164
  8.7 5.3 %copy-start.12 = (pred[256]{0:T(512)(128)(4,1)}, pred[256]{0:T(512)(128)(4,1)S(1)}, u32[]{:S(2)}) copy-start(pred[256]{0:T(512)(128)(4,1)S(1)} %compare_and_fusion.1) | copy-start | bytes 772
  10.6 4.1 %copy-start.6 = (bf16[256,256]{1,0:T(8,128)(2,1)}, bf16[256,256]{1,0:T(8,128)(2,1)S(1)}, u32[]{:S(2)}) copy-start(bf16[256,256]{1,0:T(8,128)(2,1)S(1)} %gather_fusion.3) | copy-start | bytes 393220
  10.9 29.8 %collective-permute-start = (bf16[256,256]{1,0:T(8,128)(2,1)S(1)}, bf16[256,256]{1,0:T(8,128)(2,1)}, u32[]{:S(2)}, u32[]{:S(2)}) collective-permute-start(bf16[256,256]{1,0:T(8,128)(2,1)S(1)} %convolution_convert_fusion.1), channel_id=1, source_target_pairs={{0,8},{8,16},{16,24},{24,0},{1,9},{9,17},{17,25},{25,1},{2,10},{10... | collective-permute-start | bytes 393224 | tf_op jit(solution)/shard_map/ppermute | solution.py:16
  11.4 29.3 %collective-permute-start.1 = (bf16[256,256]{1,0:T(8,128)(2,1)S(1)}, bf16[256,256]{1,0:T(8,128)(2,1)}, u32[]{:S(2)}, u32[]{:S(2)}) collective-permute-start(bf16[256,256]{1,0:T(8,128)(2,1)S(1)} %convolution_convert_fusion.1), channel_id=1, source_target_pairs={{8,0},{16,8},{24,16},{0,24},{9,1},{17,9},{25,17},{1,25},{10,2},{18... | collective-permute-start | bytes 393224 | tf_op jit(solution)/shard_map/ppermute | solution.py:18
  15.3 10.8 %copy-start.2 = (bf16[256,256]{1,0:T(8,128)(2,1)S(1)}, bf16[256,256]{1,0:T(8,128)(2,1)}, u32[]{:S(2)}) copy-start(bf16[256,256]{1,0:T(8,128)(2,1)} %param.23) | copy-start | bytes 393220
  16.3 21.1 %all-to-all-start = ((bf16[8,128,256]{2,1,0:T(8,128)(2,1)}), bf16[8,128,256]{2,1,0:T(8,128)(2,1)S(1)}, u32[]{:S(2)}, u32[]{:S(2)}) async-start(bf16[8,128,256]{2,1,0:T(8,128)(2,1)} %select_select_fusion), calls=%async_computation | async-start | bytes 1048576 | tf_op jit(solution)/shard_map/all_to_all | solution.py:77
  26.1 7.2 %copy-start.17 = (s32[40]{0:T(128)S(1)}, s32[40]{0:T(128)}, u32[]{:S(2)}) copy-start(s32[40]{0:T(128)} %get-tuple-element.51) | copy-start | bytes 484
  26.1 7.2 %copy-start.14 = (pred[40]{0:T(512)(128)(4,1)S(1)}, pred[40]{0:T(512)(128)(4,1)}, u32[]{:S(2)}) copy-start(pred[40]{0:T(512)(128)(4,1)} %iota_compare_fusion.1) | copy-start | bytes 124
  26.1 7.2 %copy-start.19 = (s32[40]{0:T(128)S(1)}, s32[40]{0:T(128)}, u32[]{:S(2)}) copy-start(s32[40]{0:T(128)} %get-tuple-element.53) | copy-start | bytes 484
  26.1 7.2 %copy-start.10 = (s32[40,2]{0,1:T(2,128)S(1)}, s32[40,2]{0,1:T(2,128)}, u32[]{:S(2)}) copy-start(s32[40,2]{0,1:T(2,128)} %param.27) | copy-start | bytes 964
  38.1 1.7 copy-start.4
  39.8 1.0 copy-start.5
  39.8 1.0 copy-start.8
  39.8 1.0 copy-start.13
  42.2 2.4 %copy-start.16 = (pred[40]{0:T(512)(128)(4,1)S(1)}, pred[40]{0:T(512)(128)(4,1)}, u32[]{:S(2)}) copy-start(pred[40]{0:T(512)(128)(4,1)} %get-tuple-element.54) | copy-start | bytes 124
  54.2 3.4 %copy-start.15 = (pred[40]{0:T(512)(128)(4,1)S(1)}, pred[40]{0:T(512)(128)(4,1)}, u32[]{:S(2)}) copy-start(pred[40]{0:T(512)(128)(4,1)} %iota_compare_fusion.1) | copy-start | bytes 124
  57.6 2.5 %copy-start.1 = (bf16[40,128,256]{2,0,1:T(8,128)(2,1)S(1)}, bf16[40,128,256]{2,0,1:T(8,128)(2,1)}, u32[]{:S(2)}) copy-start(bf16[40,128,256]{2,0,1:T(8,128)(2,1)} %copy.23) | copy-start | bytes 7864324
  60.1 5.9 %copy-start.18 = (s32[256]{0:T(256)S(1)}, s32[256]{0:T(256)}, u32[]{:S(2)}) copy-start(s32[256]{0:T(256)} %scatter_custom_fusion.1) | copy-start | bytes 3076
  60.7 19.4 %copy-start.20 = (s32[1,8]{1,0:T(1,128)S(1)}, s32[1,8]{1,0:T(1,128)}, u32[]{:S(2)}) copy-start(s32[1,8]{1,0:T(1,128)} %param.29) | copy-start | bytes 100
  61.6 19.0 %copy-start.7 = (bf16[256,256]{1,0:T(8,128)(2,1)S(1)}, bf16[256,256]{1,0:T(8,128)(2,1)}, u32[]{:S(2)}) copy-start(bf16[256,256]{1,0:T(8,128)(2,1)} %copy-done.6) | copy-start | bytes 393220
  61.6 18.5 %all-to-all-start.1 = ((bf16[8,128,256]{2,1,0:T(8,128)(2,1)}), bf16[8,128,256]{2,1,0:T(8,128)(2,1)S(1)}, u32[]{:S(2)}, u32[]{:S(2)}) async-start(bf16[8,128,256]{2,1,0:T(8,128)(2,1)} %copy.24), calls=%async_computation.1 | async-start | bytes 1048576 | tf_op jit(solution)/shard_map/all_to_all | solution.py:117
  65.9 84.5 %all-reduce.3.cloned.1.call-start = ((), (), s32[]{:S(2)}) async-start(), calls=%async_computation.2 | async-start | bytes 524288 | tf_op jit(solution)/shard_map/psum | solution.py:128
  66.3 14.2 %collective-permute-start.2 = (bf16[256,256]{1,0:T(8,128)(2,1)S(1)}, bf16[256,256]{1,0:T(8,128)(2,1)S(1)}, u32[]{:S(2)}, u32[]{:S(2)}) collective-permute-start(bf16[256,256]{1,0:T(8,128)(2,1)S(1)} %get-tuple-element.46), channel_id=1, source_target_pairs={{0,8},{8,16},{16,24},{24,0},{1,9},{9,17},{17,25},{25,1},{2,10},{10... | collective-permute-start | bytes 393224 | tf_op jit(solution)/shard_map/ppermute | solution.py:16
  66.4 14.1 %collective-permute-start.3 = (bf16[256,256]{1,0:T(8,128)(2,1)S(1)}, bf16[256,256]{1,0:T(8,128)(2,1)S(1)}, u32[]{:S(2)}, u32[]{:S(2)}) collective-permute-start(bf16[256,256]{1,0:T(8,128)(2,1)S(1)} %get-tuple-element.47), channel_id=1, source_target_pairs={{8,0},{16,8},{24,16},{0,24},{9,1},{17,9},{25,17},{1,25},{10,2},{18... | collective-permute-start | bytes 393224 | tf_op jit(solution)/shard_map/ppermute | solution.py:18
  81.6 102.6 %all-reduce.5.cloned.1.call-start = ((), (), s32[]{:S(2)}) async-start(), calls=%async_computation.3 | async-start | bytes 524288 | tf_op jit(solution)/shard_map/psum | solution.py:128
Sparse Core Ops, SparseCore 0:
  81.7 68.6 all-reduce.2
  152.9 31.2 all-reduce.4
